TPU v7x, 512 devices: a whole 4x8x8 slice. The times are simulated.
512 devices in a mesh: wide: 32 (over z, x), tensor: 16 (over y, core).
Axes of the slice: x: 4, y: 8, z: 8, core: 2. Of those that a mesh axis runs over, the one named last changes fastest.
Arguments:
- tokens: bfloat16 [16384, 8192], P('wide', 'tensor'), may hold values from -6 to 6
- key_value_weight: bfloat16 [8192, 2048], P(None, 'tensor'), may hold values from -0.0625 to 0.0625
- adapter_down_maps: bfloat16 [8192, 512, 64], P('tensor', 'wide'), may hold values from -0.0625 to 0.0625
- adapter_up_maps: bfloat16 [512, 64, 2048], P('wide', None, 'tensor'), may hold values from -0.75 to 0.75
- adapter_per_row: int32 [16384], P('wide'), may hold values from 0 to 511, as said below
- adapter_storage_slot: int32 [512], replicated, may hold values from 0 to 511, as said below
Outputs:
- kv_out: bfloat16 [16384, 2048], P('wide', 'tensor')
Inputs may be any that keep to these rules, and one draw needn't show every extreme that they name: `adapter_per_row`: the adapter stored at position p belongs to owner p // 16 of wide. Among the 512 rows of one index of wide, at most 32 name adapters of one owner; in every draw one owner gets exactly 32 rows from every index of wide. `adapter_storage_slot`: each position is taken by exactly one adapter.
All inputs are finite; a program needn't handle non-finite values.
Results may differ from a plain program's by a relative error of at most 0.0049.
Values may be sent and summed in bfloat16 or wider, within the bound.
No kernel may reach another device: no remote copies, remote signals or barrier semaphores. Data moves between devices by JAX's collectives and lax.ppermute only.
A program may use at most 64 MiB of HBM per device.

v0:
```python
import jax
import jax.numpy as jnp
from jax import lax
from jax.sharding import PartitionSpec as P


def body(
    tokens,
    key_value_weight,
    adapter_down_maps,
    adapter_up_maps,
    adapter_per_row,
    adapter_storage_slot,
):
    row_count, feature_portion = tokens.shape
    wide_count = lax.axis_size("wide")
    tensor_count = lax.axis_size("tensor")
    capacity = 2 * row_count // wide_count
    present_adapters = adapter_down_maps.shape[1]
    rank_dimension = adapter_down_maps.shape[2]
    column_portion = key_value_weight.shape[1]
    total_adapters = adapter_storage_slot.shape[0]
    slot_count = wide_count * capacity
    lane = 128
    info_rows = 8
    gathered = lax.all_gather(tokens, "tensor", axis=1, tiled=True)
    base_projection_output = jnp.dot(gathered, key_value_weight, preferred_element_type=jnp.float32)
    adapter_match = (
        adapter_per_row[:, None] == jnp.arange(total_adapters, dtype=jnp.int32)[None, :]
    ).astype(jnp.bfloat16)
    slot_parts = jnp.stack(
        [adapter_storage_slot // present_adapters, adapter_storage_slot % present_adapters], axis=1
    ).astype(jnp.bfloat16)
    picked = jnp.dot(adapter_match, slot_parts, preferred_element_type=jnp.float32)
    owner_index = picked[:, 0].astype(jnp.int32)
    local_index = picked[:, 1].astype(jnp.int32)
    owner_onehot = (
        owner_index[:, None] == jnp.arange(wide_count, dtype=jnp.int32)[None, :]
    ).astype(jnp.float32)
    row_iota = jnp.arange(row_count, dtype=jnp.int32)
    strictly_before = (row_iota[:, None] > row_iota[None, :]).astype(jnp.float32)
    earlier = jnp.dot(strictly_before, owner_onehot, preferred_element_type=jnp.float32)
    rank_in_owner = jnp.sum(earlier * owner_onehot, axis=1).astype(jnp.int32)
    destination = owner_index * capacity + rank_in_owner
    placement = (jnp.arange(slot_count, dtype=jnp.int32)[:, None] == destination[None, :]).astype(
        jnp.bfloat16
    )
    lane_tiles = feature_portion // lane
    local_code = jnp.broadcast_to(
        (local_index + 1).astype(jnp.bfloat16)[:, None], (row_count, lane)
    )
    placement_blocks = placement.reshape(wide_count, capacity, row_count)
    token_tiles = tokens.reshape(row_count, lane_tiles, lane)
    placed = jnp.einsum(
        "dcr,rjl->djcl", placement_blocks, token_tiles, preferred_element_type=jnp.float32
    ).astype(jnp.bfloat16)
    pieces = [placed.reshape(wide_count, lane_tiles * capacity, lane)]
    placed_code = jnp.dot(placement, local_code, preferred_element_type=jnp.float32)
    slot_code = placed_code[:, 0].astype(jnp.bfloat16).reshape(wide_count, 1, capacity)
    pieces.append(jnp.pad(slot_code, ((0, 0), (0, info_rows - 1), (0, lane - capacity))))
    send_block = jnp.concatenate(pieces, axis=1)
    got_block = lax.all_to_all(send_block, "wide", split_axis=0, concat_axis=0, tiled=True)
    flat_rows = jnp.concatenate(
        [
            got_block[:, tile * capacity : (tile + 1) * capacity, :].reshape(slot_count, lane)
            for tile in range(lane_tiles)
        ],
        axis=1,
    )
    got_code = got_block[:, lane_tiles * capacity, :capacity].reshape(slot_count).astype(jnp.int32)
    selected = (got_code[:, None] == jnp.arange(1, present_adapters + 1, dtype=jnp.int32)[None, :])[
        :, :, None
    ]
    down_matrix = adapter_down_maps.reshape(feature_portion, present_adapters * rank_dimension)
    all_ranks = jnp.dot(flat_rows, down_matrix, preferred_element_type=jnp.float32)
    all_ranks = all_ranks.reshape(slot_count, present_adapters, rank_dimension)
    partial_value = jnp.sum(jnp.where(selected, all_ranks, 0.0), axis=1)
    block_rows = slot_count // tensor_count
    dense_shape = (tensor_count, block_rows * rank_dimension // 128, 128)
    slot_blocks = partial_value.reshape(dense_shape)
    gathered_blocks = lax.all_to_all(slot_blocks, "tensor", split_axis=0, concat_axis=0, tiled=True)
    own_sum = jnp.sum(gathered_blocks, axis=0).astype(jnp.bfloat16)
    spread_shape = (tensor_count, 16, block_rows * rank_dimension // 16)
    spread = jnp.broadcast_to(own_sum.reshape(spread_shape[1:])[None], spread_shape)
    reduced_rows = lax.all_to_all(spread, "tensor", split_axis=0, concat_axis=0, tiled=True)
    reduced_rows = reduced_rows.reshape(slot_count, rank_dimension)
    base_tie = (base_projection_output[0, 0] * 0.0).astype(jnp.bfloat16)
    expanded_rows = jnp.where(
        selected, reduced_rows[:, None, :] + base_tie, jnp.zeros((), jnp.bfloat16)
    ).reshape(slot_count, present_adapters * rank_dimension)
    up_matrix = adapter_up_maps.reshape(present_adapters * rank_dimension, column_portion)
    adapter_correction = jnp.dot(
        expanded_rows, up_matrix, preferred_element_type=jnp.float32
    ).astype(jnp.bfloat16)
    adapter_correction = adapter_correction.reshape(wide_count, capacity, column_portion)
    returned_rows = lax.all_to_all(
        adapter_correction, "wide", split_axis=0, concat_axis=0, tiled=True
    )
    returned_rows = returned_rows.reshape(slot_count, column_portion)
    adapter_row_output = jnp.dot(placement.T, returned_rows, preferred_element_type=jnp.float32)
    return (base_projection_output + adapter_row_output).astype(jnp.bfloat16)


def solution(mesh):
    in_specs = (
        P("wide", "tensor"),
        P(None, "tensor"),
        P("tensor", "wide", None),
        P("wide", None, "tensor"),
        P("wide"),
        P(),
    )
    out_specs = P("wide", "tensor")
    return jax.shard_map(body, mesh=mesh, in_specs=in_specs, out_specs=out_specs, check_vma=False)
```

profile of v0, /device:TPU:1, one launch (start us, length us, event | category | flops | bytes accessed | tf_op | source)
XLA Modules:
  0.0 120.1 jit_solution(7140281131898327111)
XLA Ops:
  6.5 0.7 all-gather.2.cloned.1.call-update
  7.3 0.8 fusion.42
  8.0 1.1 fusion.35
  9.1 0.3 fusion.20
  9.4 0.6 fusion.4
  10.2 0.8 fusion.9
  10.9 1.2 fusion.21
  12.1 13.7 %all-to-all-start = ((bf16[32,136,128]{2,1,0:T(8,128)(2,1)}), bf16[32,136,128]{2,1,0:T(8,128)(2,1)S(1)}, u32[]{:S(2)}, u32[]{:S(2)}) async-start(bf16[32,136,128]{2,1,0:T(8,128)(2,1)} %fusion.21), calls=%async_computation | async-start | bytes 2228224 | tf_op jit(solution)/shard_map/all_to_all | solution.py:62
  25.8 27.3 %all-to-all-done = bf16[32,136,128]{2,1,0:T(8,128)(2,1)S(1)} async-done(((bf16[32,136,128]{2,1,0:T(8,128)(2,1)}), bf16[32,136,128]{2,1,0:T(8,128)(2,1)S(1)}, u32[]{:S(2)}, u32[]{:S(2)}) %all-to-all-start) | async-done | bytes 1114144 | tf_op jit(solution)/shard_map/all_to_all | solution.py:62
  53.5 1.0 copy-done.2
  54.5 1.3 %select_reduce_fusion = f32[1024,64]{0,1:T(8,128)S(1)} fusion(pred[1024,16]{0,1:T(8,128)(4,1)S(1)} %broadcast_compare_fusion, bf16[1024,128]{1,0:T(8,128)(2,1)S(1)} %bitcast.51, bf16[1024,128]{1,0:T(8,128)(2,1)S(1)} %bitcast.52, bf16[1024,128]{1,0:T(8,128)(2,1)S(1)} %bitcast.53, bf16[1024,128]{1,0:T(8,128)(2,1)S(1)} %bitcast.50, ...), kind=kOutput, calls=%fused_computation | convolution fusion | flops 1079967744 | bytes 2375680 | tf_op jit(solution)/shard_map/dot_general | solution.py:75
  55.8 0.2 copy.14
  56.0 0.1 reshape.141
  56.2 23.4 %all_to_all.20 = f32[16,32,128]{2,1,0:T(8,128)S(1)} all-to-all(f32[16,32,128]{2,1,0:T(8,128)S(1)} %reshape.141), channel_id=1, replica_groups=mesh['wide'=32,'tensor'=16] {'tensor'}, dimensions={0} | all-to-all | bytes 524288 | tf_op jit(solution)/shard_map/all_to_all | solution.py:81
  79.6 0.7 broadcast_in_dim.58
  80.2 3.4 %all-to-all-start.2 = ((bf16[16,16,256]{2,1,0:T(8,128)(2,1)}), bf16[16,16,256]{2,1,0:T(8,128)(2,1)S(1)}, u32[]{:S(2)}, u32[]{:S(2)}) async-start(bf16[16,16,256]{2,1,0:T(8,128)(2,1)} %broadcast_in_dim.58), calls=%async_computation.2 | async-start | bytes 262144 | tf_op jit(solution)/shard_map/all_to_all | solution.py:85
  83.7 5.7 %fusion.55 = f32[512,128]{1,0:T(8,128)S(1)} fusion(bf16[512,8192]{1,0:T(8,128)(2,1)} %all-gather.2.cloned.1.call-done, bf16[8192,128]{1,0:T(8,128)(2,1)S(1)} %copy-done), kind=kOutput, calls=%fused_computation.75 | convolution fusion | flops 1073741824 | bytes 10747904 | tf_op jit(solution)/shard_map/dot_general | solution.py:27
  89.5 0.6 slice.45
  90.8 1.4 %all-to-all-done.2 = bf16[16,16,256]{2,1,0:T(8,128)(2,1)S(1)} async-done(((bf16[16,16,256]{2,1,0:T(8,128)(2,1)}), bf16[16,16,256]{2,1,0:T(8,128)(2,1)S(1)}, u32[]{:S(2)}, u32[]{:S(2)}) %all-to-all-start.2) | async-done | bytes 131104 | tf_op jit(solution)/shard_map/all_to_all | solution.py:85
  92.1 0.2 add.55
  92.3 0.1 copy.15
  92.5 0.8 fusion.15
  93.2 18.7 %all_to_all.21 = bf16[32,32,128]{2,1,0:T(8,128)(2,1)S(1)} all-to-all(bf16[32,32,128]{2,1,0:T(8,128)(2,1)S(1)} %bitcast.49), channel_id=1, replica_groups=mesh['wide'=32,'tensor'=16] {'wide'}, dimensions={0} | all-to-all | bytes 524288 | tf_op jit(solution)/shard_map/all_to_all | solution.py:96
  111.9 1.4 %fusion.19 = bf16[512,128]{1,0:T(8,128)(2,1)} fusion(f32[512,128]{1,0:T(8,128)S(1)} %fusion.55, bf16[1024,128]{1,0:T(8,128)(2,1)S(1)} %bitcast.48, s32[512]{0:T(512)S(1)} %convert_add_fusion), kind=kOutput, calls=%fused_computation.16 | convolution fusion | flops 134873088 | bytes 657408 | tf_op jit(solution)/shard_map/dot_general | solution.py:100
  (26 shorter events, 0.6 us)
Async XLA Ops:
  6.5 77.2 %copy-start = (bf16[8192,128]{1,0:T(8,128)(2,1)S(1)}, bf16[8192,128]{1,0:T(8,128)(2,1)}, u32[]{:S(2)}) copy-start(bf16[8192,128]{1,0:T(8,128)(2,1)} %param.7) | copy-start | bytes 6291460
  6.5 3.6 %copy-start.1 = (bf16[512,512]{1,0:T(8,128)(2,1)S(1)}, bf16[512,512]{1,0:T(8,128)(2,1)}, u32[]{:S(2)}) copy-start(bf16[512,512]{1,0:T(8,128)(2,1)} %param.6) | copy-start | bytes 1572868
  6.5 77.2 %all-gather.2.cloned.1.call-start = ((), (), s32[]{:S(2)}) async-start(), calls=%async_computation.4 | async-start | bytes 8912896 | tf_op jit(solution)/shard_map/all_gather | solution.py:26
  12.1 41.1 %all-to-all-start = ((bf16[32,136,128]{2,1,0:T(8,128)(2,1)}), bf16[32,136,128]{2,1,0:T(8,128)(2,1)S(1)}, u32[]{:S(2)}, u32[]{:S(2)}) async-start(bf16[32,136,128]{2,1,0:T(8,128)(2,1)} %fusion.21), calls=%async_computation | async-start | bytes 2228224 | tf_op jit(solution)/shard_map/all_to_all | solution.py:62
  53.3 1.2 %copy-start.2 = (bf16[512,16,64]{0,2,1:T(8,128)(2,1)S(1)}, bf16[512,16,64]{0,2,1:T(8,128)(2,1)}, u32[]{:S(2)}) copy-start(bf16[512,16,64]{0,2,1:T(8,128)(2,1)} %param.8) | copy-start | bytes 3145732
  80.2 11.9 %all-to-all-start.2 = ((bf16[16,16,256]{2,1,0:T(8,128)(2,1)}), bf16[16,16,256]{2,1,0:T(8,128)(2,1)S(1)}, u32[]{:S(2)}, u32[]{:S(2)}) async-start(bf16[16,16,256]{2,1,0:T(8,128)(2,1)} %broadcast_in_dim.58), calls=%async_computation.2 | async-start | bytes 262144 | tf_op jit(solution)/shard_map/all_to_all | solution.py:85
  83.7 8.8 %copy-start.3 = (bf16[16,64,128]{2,1,0:T(8,128)(2,1)S(1)}, bf16[16,64,128]{2,1,0:T(8,128)(2,1)}, u32[]{:S(2)}) copy-start(bf16[16,64,128]{2,1,0:T(8,128)(2,1)} %param.9) | copy-start | bytes 786436
Sparse Core Ops, SparseCore 0:
  9.5 67.3 all-gather.1
where the time goes:
time: 121 us; the launch traced here: 120 us
  blocking collectives  42 us (35%)
  waiting for transfers between devices  29.4 us (24%)
  starting transfers between devices  17.1 us (14%)
  between operations  14.3 us (12%)
  matrix products  11.9 us (10%)
  local copies, waits for them, and re-layouts  3.23 us (3%)
  other arithmetic  2.17 us (2%)
    all_to_all x1, waiting for transfers between devices, body(): lax.all_to_all(send_block, 'wide', split_axis=0, concat_axis=0, tiled=True)  27.3 us
    all_to_all x1, blocking collectives, body(): lax.all_to_all(slot_blocks, 'tensor', split_axis=0, concat_axis=0, tiled=...  23.4 us
    all_to_all x1, blocking collectives, body(): lax.all_to_all(adapter_correction, 'wide', split_axis=0, concat_axis=0, t...  18.7 us
    all_to_all x1, starting transfers between devices, body(): lax.all_to_all(send_block, 'wide', split_axis=0, concat_axis=0, tiled=True)  13.7 us
    dot_general x1, matrix products, body(): jnp.dot(gathered, key_value_weight, preferred_element_type=jnp.float32)  5.74 us
    all_to_all x1, starting transfers between devices, body(): lax.all_to_all(spread, 'tensor', split_axis=0, concat_axis=0, tiled=True)  3.41 us
  transfers between devices with their start and end apart: 3, of which 2 were waited for; matrix products, arithmetic and copies ran while one was open for 11% of the time, Pallas kernels for 0%

commit v1 on v0

--- a/solution.py
+++ b/solution.py
@@ -2,6 +2,21 @@
 import jax.numpy as jnp
 from jax import lax
 from jax.sharding import PartitionSpec as P
+
+
+def follow_units(in_array, in_dim, load):
+    y2, then = (in_array.shape[:in_dim], in_array.shape[in_dim + 1 :])
+    return jnp.moveaxis(in_array.reshape(*y2, load, -1, *then), in_dim, 0)
+
+
+def records_turn(block_here, array_axis):
+    block_here = jnp.moveaxis(block_here, 0, array_axis)
+    row_out = block_here.shape
+    return block_here.reshape(
+        *row_out[:array_axis],
+        row_out[array_axis] * row_out[array_axis + 1],
+        *row_out[array_axis + 2 :]
+    )
 
 
 def body(
@@ -12,6 +27,20 @@
     adapter_per_row,
     adapter_storage_slot,
 ):
+
+    def panel_list(u, group_axis, x_local, frame_in):
+        p_next = lax.axis_index(group_axis)
+        piece_out = lax.axis_size(group_axis)
+        odd, e_now = (piece_out, p_next)
+        local_now = follow_units(u, x_local, odd)
+        found = [local_now[e_now]]
+        for p in tuple(range(1, odd)):
+            built = local_now[e_now ^ p]
+            field_out = lax.ppermute(built, group_axis, [(t, t ^ p) for t in range(odd)])
+            found.append(field_out)
+        local_now = jnp.stack(found, axis=0)[e_now ^ jnp.arange(odd)]
+        return records_turn(local_now, frame_in)
+
     row_count, feature_portion = tokens.shape
     wide_count = lax.axis_size("wide")
     tensor_count = lax.axis_size("tensor")
@@ -82,7 +111,7 @@
     own_sum = jnp.sum(gathered_blocks, axis=0).astype(jnp.bfloat16)
     spread_shape = (tensor_count, 16, block_rows * rank_dimension // 16)
     spread = jnp.broadcast_to(own_sum.reshape(spread_shape[1:])[None], spread_shape)
-    reduced_rows = lax.all_to_all(spread, "tensor", split_axis=0, concat_axis=0, tiled=True)
+    reduced_rows = panel_list(spread, "tensor", 0, 0)
     reduced_rows = reduced_rows.reshape(slot_count, rank_dimension)
     base_tie = (base_projection_output[0, 0] * 0.0).astype(jnp.bfloat16)
     expanded_rows = jnp.where(

time: 121 us -> 175 us (1.45); the launches traced: 120 us -> 171 us
  starting transfers between devices: 17.1 us -> 78.1 us
  blocking collectives: 42 us -> 19.1 us
  waiting for transfers between devices: 29.4 us -> 41.8 us
    ppermute x0 -> x15, starting transfers between devices: none -> 54.2 us  [panel_list(): lax.ppermute(built, group_axis, [(t, t ^ p) for t in range(odd)])]
    all_to_all x1 -> x0, blocking collectives: 23.4 us -> none  [body(): lax.all_to_all(slot_blocks, 'tensor', split_axis=0, concat_axis=0, tiled=...]
    all_to_all x1, waiting for transfers between devices: 1.37 us -> 12.4 us  [body(): lax.all_to_all(slot_blocks, 'tensor', split_axis=0, concat_axis=0, tiled=...]
    all_to_all x1, starting transfers between devices: 3.41 us -> 10.2 us  [body(): lax.all_to_all(slot_blocks, 'tensor', split_axis=0, concat_axis=0, tiled=...]
  transfers between devices with their start and end apart: 3 -> 18, of which waited for: 2 -> 3; matrix products, arithmetic and copies ran while one was open for 11% -> 5% of each run, Pallas kernels for 0% -> 0%
where the time goes in v1:
time: 175 us; the launch traced here: 171 us
  starting transfers between devices  78.1 us (45%)
  waiting for transfers between devices  41.8 us (24%)
  blocking collectives  19.1 us (11%)
  between operations  14.6 us (8%)
  matrix products  11.9 us (7%)
  local copies, waits for them, and re-layouts  3.85 us (2%)
  other arithmetic  2.19 us (1%)
    ppermute x15, starting transfers between devices, panel_list(): lax.ppermute(built, group_axis, [(t, t ^ p) for t in range(odd)])  54.2 us
    all_to_all x1, waiting for transfers between devices, body(): lax.all_to_all(send_block, 'wide', split_axis=0, concat_axis=0, tiled=True)  27.3 us
    all_to_all x1, blocking collectives, body(): lax.all_to_all(adapter_correction, 'wide', split_axis=0, concat_axis=0, t...  19.1 us
    all_to_all x1, starting transfers between devices, body(): lax.all_to_all(send_block, 'wide', split_axis=0, concat_axis=0, tiled=True)  13.7 us
    all_to_all x1, waiting for transfers between devices, body(): lax.all_to_all(slot_blocks, 'tensor', split_axis=0, concat_axis=0, tiled=...  12.4 us
    all_to_all x1, starting transfers between devices, body(): lax.all_to_all(slot_blocks, 'tensor', split_axis=0, concat_axis=0, tiled=...  10.2 us
    dot_general x1, matrix products, body(): jnp.dot(gathered, key_value_weight, preferred_element_type=jnp.float32)  5.74 us
  transfers between devices with their start and end apart: 18, of which 3 were waited for; matrix products, arithmetic and copies ran while one was open for 5% of the time, Pallas kernels for 0%

profile of v1, /device:TPU:1, one launch (start us, length us, event | category | flops | bytes accessed | tf_op | source)
XLA Modules:
  0.0 171.4 jit_solution(8080477796267139494)
XLA Ops:
  12.1 13.7 %all-to-all-start = ((bf16[32,136,128]{2,1,0:T(8,128)(2,1)}), bf16[32,136,128]{2,1,0:T(8,128)(2,1)S(1)}, u32[]{:S(2)}, u32[]{:S(2)}) async-start(bf16[32,136,128]{2,1,0:T(8,128)(2,1)} %fusion.21), calls=%async_computation | async-start | bytes 2228224 | tf_op jit(solution)/shard_map/all_to_all | solution.py:91
  25.8 27.3 %all-to-all-done = bf16[32,136,128]{2,1,0:T(8,128)(2,1)S(1)} async-done(((bf16[32,136,128]{2,1,0:T(8,128)(2,1)}), bf16[32,136,128]{2,1,0:T(8,128)(2,1)S(1)}, u32[]{:S(2)}, u32[]{:S(2)}) %all-to-all-start) | async-done | bytes 1114144 | tf_op jit(solution)/shard_map/all_to_all | solution.py:91
  54.5 1.3 select_reduce_fusion
  56.9 10.2 %all-to-all-start.1 = ((f32[16,32,128]{2,1,0:T(8,128)}), f32[16,32,128]{2,1,0:T(8,128)S(1)}, u32[]{:S(2)}, u32[]{:S(2)}) async-start(f32[16,32,128]{2,1,0:T(8,128)} %reshape.203), calls=%async_computation.1 | async-start | bytes 524288 | tf_op jit(solution)/shard_map/all_to_all | solution.py:110
  67.1 12.4 %all-to-all-done.1 = f32[16,32,128]{2,1,0:T(8,128)S(1)} async-done(((f32[16,32,128]{2,1,0:T(8,128)}), f32[16,32,128]{2,1,0:T(8,128)S(1)}, u32[]{:S(2)}, u32[]{:S(2)}) %all-to-all-start.1) | async-done | bytes 262176 | tf_op jit(solution)/shard_map/all_to_all | solution.py:110
  79.6 1.9 %collective-permute-start = (bf16[1,16,256]{2,1,0:T(8,128)(2,1)S(1)}, bf16[1,16,256]{2,1,0:T(8,128)(2,1)S(1)}, u32[]{:S(2)}, u32[]{:S(2)}) collective-permute-start(bf16[1,16,256]{2,1,0:T(8,128)(2,1)S(1)} %convert_element_type.102), channel_id=1, source_target_pairs={{0,1},{1,0},{2,3},{3,2},{4,5},{5,4},{6,7},{7,6},{8,9},{9,8},{10,11... | collective-permute-start | bytes 24584 | tf_op jit(solution)/shard_map/ppermute | solution.py:39
  81.5 1.9 %collective-permute-start.1 = (bf16[1,16,256]{2,1,0:T(8,128)(2,1)S(1)}, bf16[1,16,256]{2,1,0:T(8,128)(2,1)S(1)}, u32[]{:S(2)}, u32[]{:S(2)}) collective-permute-start(bf16[1,16,256]{2,1,0:T(8,128)(2,1)S(1)} %convert_element_type.102), channel_id=1, source_target_pairs={{0,2},{1,3},{2,0},{3,1},{4,6},{5,7},{6,4},{7,5},{8,10},{9,11},{10,... | collective-permute-start | bytes 24584 | tf_op jit(solution)/shard_map/ppermute | solution.py:39
  83.5 4.0 %collective-permute-start.2 = (bf16[1,16,256]{2,1,0:T(8,128)(2,1)S(1)}, bf16[1,16,256]{2,1,0:T(8,128)(2,1)S(1)}, u32[]{:S(2)}, u32[]{:S(2)}) collective-permute-start(bf16[1,16,256]{2,1,0:T(8,128)(2,1)S(1)} %convert_element_type.102), channel_id=1, source_target_pairs={{0,3},{1,2},{2,1},{3,0},{4,7},{5,6},{6,5},{7,4},{8,11},{9,10},{10,... | collective-permute-start | bytes 24584 | tf_op jit(solution)/shard_map/ppermute | solution.py:39
  87.5 2.2 %collective-permute-start.3 = (bf16[1,16,256]{2,1,0:T(8,128)(2,1)S(1)}, bf16[1,16,256]{2,1,0:T(8,128)(2,1)S(1)}, u32[]{:S(2)}, u32[]{:S(2)}) collective-permute-start(bf16[1,16,256]{2,1,0:T(8,128)(2,1)S(1)} %convert_element_type.102), channel_id=1, source_target_pairs={{0,4},{1,5},{2,6},{3,7},{4,0},{5,1},{6,2},{7,3},{8,12},{9,13},{10,... | collective-permute-start | bytes 24584 | tf_op jit(solution)/shard_map/ppermute | solution.py:39
  89.7 3.9 %collective-permute-start.4 = (bf16[1,16,256]{2,1,0:T(8,128)(2,1)S(1)}, bf16[1,16,256]{2,1,0:T(8,128)(2,1)S(1)}, u32[]{:S(2)}, u32[]{:S(2)}) collective-permute-start(bf16[1,16,256]{2,1,0:T(8,128)(2,1)S(1)} %convert_element_type.102), channel_id=1, source_target_pairs={{0,5},{1,4},{2,7},{3,6},{4,1},{5,0},{6,3},{7,2},{8,13},{9,12},{10,... | collective-permute-start | bytes 24584 | tf_op jit(solution)/shard_map/ppermute | solution.py:39
  93.6 3.0 %collective-permute-start.5 = (bf16[1,16,256]{2,1,0:T(8,128)(2,1)S(1)}, bf16[1,16,256]{2,1,0:T(8,128)(2,1)S(1)}, u32[]{:S(2)}, u32[]{:S(2)}) collective-permute-start(bf16[1,16,256]{2,1,0:T(8,128)(2,1)S(1)} %convert_element_type.102), channel_id=1, source_target_pairs={{0,6},{1,7},{2,4},{3,5},{4,2},{5,3},{6,0},{7,1},{8,14},{9,15},{10,... | collective-permute-start | bytes 24584 | tf_op jit(solution)/shard_map/ppermute | solution.py:39
  96.6 4.7 %collective-permute-start.6 = (bf16[1,16,256]{2,1,0:T(8,128)(2,1)S(1)}, bf16[1,16,256]{2,1,0:T(8,128)(2,1)S(1)}, u32[]{:S(2)}, u32[]{:S(2)}) collective-permute-start(bf16[1,16,256]{2,1,0:T(8,128)(2,1)S(1)} %convert_element_type.102), channel_id=1, source_target_pairs={{0,7},{1,6},{2,5},{3,4},{4,3},{5,2},{6,1},{7,0},{8,15},{9,14},{10,... | collective-permute-start | bytes 24584 | tf_op jit(solution)/shard_map/ppermute | solution.py:39
  101.4 2.7 %collective-permute-start.7 = (bf16[1,16,256]{2,1,0:T(8,128)(2,1)S(1)}, bf16[1,16,256]{2,1,0:T(8,128)(2,1)S(1)}, u32[]{:S(2)}, u32[]{:S(2)}) collective-permute-start(bf16[1,16,256]{2,1,0:T(8,128)(2,1)S(1)} %convert_element_type.102), channel_id=1, source_target_pairs={{0,8},{1,9},{2,10},{3,11},{4,12},{5,13},{6,14},{7,15},{8,0},{9,1},... | collective-permute-start | bytes 24584 | tf_op jit(solution)/shard_map/ppermute | solution.py:39
  104.2 6.4 %collective-permute-start.8 = (bf16[1,16,256]{2,1,0:T(8,128)(2,1)S(1)}, bf16[1,16,256]{2,1,0:T(8,128)(2,1)S(1)}, u32[]{:S(2)}, u32[]{:S(2)}) collective-permute-start(bf16[1,16,256]{2,1,0:T(8,128)(2,1)S(1)} %convert_element_type.102), channel_id=1, source_target_pairs={{0,9},{1,8},{2,11},{3,10},{4,13},{5,12},{6,15},{7,14},{8,1},{9,0},... | collective-permute-start | bytes 24584 | tf_op jit(solution)/shard_map/ppermute | solution.py:39
  110.6 1.9 %collective-permute-start.9 = (bf16[1,16,256]{2,1,0:T(8,128)(2,1)S(1)}, bf16[1,16,256]{2,1,0:T(8,128)(2,1)S(1)}, u32[]{:S(2)}, u32[]{:S(2)}) collective-permute-start(bf16[1,16,256]{2,1,0:T(8,128)(2,1)S(1)} %convert_element_type.102), channel_id=1, source_target_pairs={{0,10},{1,11},{2,8},{3,9},{4,14},{5,15},{6,12},{7,13},{8,2},{9,3},... | collective-permute-start | bytes 24584 | tf_op jit(solution)/shard_map/ppermute | solution.py:39
  112.5 7.0 %collective-permute-start.10 = (bf16[1,16,256]{2,1,0:T(8,128)(2,1)S(1)}, bf16[1,16,256]{2,1,0:T(8,128)(2,1)S(1)}, u32[]{:S(2)}, u32[]{:S(2)}) collective-permute-start(bf16[1,16,256]{2,1,0:T(8,128)(2,1)S(1)} %convert_element_type.102), channel_id=1, source_target_pairs={{0,11},{1,10},{2,9},{3,8},{4,15},{5,14},{6,13},{7,12},{8,3},{9,2},... | collective-permute-start | bytes 24584 | tf_op jit(solution)/shard_map/ppermute | solution.py:39
  119.6 1.9 %collective-permute-start.11 = (bf16[1,16,256]{2,1,0:T(8,128)(2,1)S(1)}, bf16[1,16,256]{2,1,0:T(8,128)(2,1)S(1)}, u32[]{:S(2)}, u32[]{:S(2)}) collective-permute-start(bf16[1,16,256]{2,1,0:T(8,128)(2,1)S(1)} %convert_element_type.102), channel_id=1, source_target_pairs={{0,12},{1,13},{2,14},{3,15},{4,8},{5,9},{6,10},{7,11},{8,4},{9,5},... | collective-permute-start | bytes 24584 | tf_op jit(solution)/shard_map/ppermute | solution.py:39
  121.5 5.4 %collective-permute-start.12 = (bf16[1,16,256]{2,1,0:T(8,128)(2,1)S(1)}, bf16[1,16,256]{2,1,0:T(8,128)(2,1)S(1)}, u32[]{:S(2)}, u32[]{:S(2)}) collective-permute-start(bf16[1,16,256]{2,1,0:T(8,128)(2,1)S(1)} %convert_element_type.102), channel_id=1, source_target_pairs={{0,13},{1,12},{2,15},{3,14},{4,9},{5,8},{6,11},{7,10},{8,5},{9,4},... | collective-permute-start | bytes 24584 | tf_op jit(solution)/shard_map/ppermute | solution.py:39
  126.9 1.9 %collective-permute-start.13 = (bf16[1,16,256]{2,1,0:T(8,128)(2,1)S(1)}, bf16[1,16,256]{2,1,0:T(8,128)(2,1)S(1)}, u32[]{:S(2)}, u32[]{:S(2)}) collective-permute-start(bf16[1,16,256]{2,1,0:T(8,128)(2,1)S(1)} %convert_element_type.102), channel_id=1, source_target_pairs={{0,14},{1,15},{2,12},{3,13},{4,10},{5,11},{6,8},{7,9},{8,6},{9,7},... | collective-permute-start | bytes 24584 | tf_op jit(solution)/shard_map/ppermute | solution.py:39
  128.9 5.2 %collective-permute-start.14 = (bf16[1,16,256]{2,1,0:T(8,128)(2,1)S(1)}, bf16[1,16,256]{2,1,0:T(8,128)(2,1)S(1)}, u32[]{:S(2)}, u32[]{:S(2)}) collective-permute-start(bf16[1,16,256]{2,1,0:T(8,128)(2,1)S(1)} %convert_element_type.102), channel_id=1, source_target_pairs={{0,15},{1,14},{2,13},{3,12},{4,11},{5,10},{6,9},{7,8},{8,7},{9,6},... | collective-permute-start | bytes 24584 | tf_op jit(solution)/shard_map/ppermute | solution.py:39
  134.2 1.2 collective-permute-done.14
  136.0 5.7 %fusion.56 = f32[512,128]{1,0:T(8,128)S(1)} fusion(bf16[512,8192]{1,0:T(8,128)(2,1)} %all-gather.2.cloned.1.call-done, bf16[8192,128]{1,0:T(8,128)(2,1)S(1)} %copy-done), kind=kOutput, calls=%fused_computation.95 | convolution fusion | flops 1073741824 | bytes 10747904 | tf_op jit(solution)/shard_map/dot_general | solution.py:56
  144.1 19.1 %all_to_all.15 = bf16[32,32,128]{2,1,0:T(8,128)(2,1)S(1)} all-to-all(bf16[32,32,128]{2,1,0:T(8,128)(2,1)S(1)} %bitcast.82), channel_id=1, replica_groups=mesh['wide'=32,'tensor'=16] {'wide'}, dimensions={0} | all-to-all | bytes 524288 | tf_op jit(solution)/shard_map/all_to_all | solution.py:125
  163.1 1.4 fusion.19
  (74 shorter events, 10.3 us)
Async XLA Ops:
  6.5 129.5 %copy-start = (bf16[8192,128]{1,0:T(8,128)(2,1)S(1)}, bf16[8192,128]{1,0:T(8,128)(2,1)}, u32[]{:S(2)}) copy-start(bf16[8192,128]{1,0:T(8,128)(2,1)} %param.7) | copy-start | bytes 6291460
  6.5 3.6 %copy-start.1 = (bf16[512,512]{1,0:T(8,128)(2,1)S(1)}, bf16[512,512]{1,0:T(8,128)(2,1)}, u32[]{:S(2)}) copy-start(bf16[512,512]{1,0:T(8,128)(2,1)} %param.6) | copy-start | bytes 1572868
  6.5 129.5 %all-gather.2.cloned.1.call-start = ((), (), s32[]{:S(2)}) async-start(), calls=%async_computation.3 | async-start | bytes 8912896 | tf_op jit(solution)/shard_map/all_gather | solution.py:55
  12.1 41.1 %all-to-all-start = ((bf16[32,136,128]{2,1,0:T(8,128)(2,1)}), bf16[32,136,128]{2,1,0:T(8,128)(2,1)S(1)}, u32[]{:S(2)}, u32[]{:S(2)}) async-start(bf16[32,136,128]{2,1,0:T(8,128)(2,1)} %fusion.21), calls=%async_computation | async-start | bytes 2228224 | tf_op jit(solution)/shard_map/all_to_all | solution.py:91
  53.3 1.2 copy-start.2
  56.9 22.6 %all-to-all-start.1 = ((f32[16,32,128]{2,1,0:T(8,128)}), f32[16,32,128]{2,1,0:T(8,128)S(1)}, u32[]{:S(2)}, u32[]{:S(2)}) async-start(f32[16,32,128]{2,1,0:T(8,128)} %reshape.203), calls=%async_computation.1 | async-start | bytes 524288 | tf_op jit(solution)/shard_map/all_to_all | solution.py:110
  79.6 14.0 %collective-permute-start = (bf16[1,16,256]{2,1,0:T(8,128)(2,1)S(1)}, bf16[1,16,256]{2,1,0:T(8,128)(2,1)S(1)}, u32[]{:S(2)}, u32[]{:S(2)}) collective-permute-start(bf16[1,16,256]{2,1,0:T(8,128)(2,1)S(1)} %convert_element_type.102), channel_id=1, source_target_pairs={{0,1},{1,0},{2,3},{3,2},{4,5},{5,4},{6,7},{7,6},{8,9},{9,8},{10,11... | collective-permute-start | bytes 24584 | tf_op jit(solution)/shard_map/ppermute | solution.py:39
  81.5 15.1 %collective-permute-start.1 = (bf16[1,16,256]{2,1,0:T(8,128)(2,1)S(1)}, bf16[1,16,256]{2,1,0:T(8,128)(2,1)S(1)}, u32[]{:S(2)}, u32[]{:S(2)}) collective-permute-start(bf16[1,16,256]{2,1,0:T(8,128)(2,1)S(1)} %convert_element_type.102), channel_id=1, source_target_pairs={{0,2},{1,3},{2,0},{3,1},{4,6},{5,7},{6,4},{7,5},{8,10},{9,11},{10,... | collective-permute-start | bytes 24584 | tf_op jit(solution)/shard_map/ppermute | solution.py:39
  83.5 17.9 %collective-permute-start.2 = (bf16[1,16,256]{2,1,0:T(8,128)(2,1)S(1)}, bf16[1,16,256]{2,1,0:T(8,128)(2,1)S(1)}, u32[]{:S(2)}, u32[]{:S(2)}) collective-permute-start(bf16[1,16,256]{2,1,0:T(8,128)(2,1)S(1)} %convert_element_type.102), channel_id=1, source_target_pairs={{0,3},{1,2},{2,1},{3,0},{4,7},{5,6},{6,5},{7,4},{8,11},{9,10},{10,... | collective-permute-start | bytes 24584 | tf_op jit(solution)/shard_map/ppermute | solution.py:39
  87.5 16.7 %collective-permute-start.3 = (bf16[1,16,256]{2,1,0:T(8,128)(2,1)S(1)}, bf16[1,16,256]{2,1,0:T(8,128)(2,1)S(1)}, u32[]{:S(2)}, u32[]{:S(2)}) collective-permute-start(bf16[1,16,256]{2,1,0:T(8,128)(2,1)S(1)} %convert_element_type.102), channel_id=1, source_target_pairs={{0,4},{1,5},{2,6},{3,7},{4,0},{5,1},{6,2},{7,3},{8,12},{9,13},{10,... | collective-permute-start | bytes 24584 | tf_op jit(solution)/shard_map/ppermute | solution.py:39
  89.7 20.9 %collective-permute-start.4 = (bf16[1,16,256]{2,1,0:T(8,128)(2,1)S(1)}, bf16[1,16,256]{2,1,0:T(8,128)(2,1)S(1)}, u32[]{:S(2)}, u32[]{:S(2)}) collective-permute-start(bf16[1,16,256]{2,1,0:T(8,128)(2,1)S(1)} %convert_element_type.102), channel_id=1, source_target_pairs={{0,5},{1,4},{2,7},{3,6},{4,1},{5,0},{6,3},{7,2},{8,13},{9,12},{10,... | collective-permute-start | bytes 24584 | tf_op jit(solution)/shard_map/ppermute | solution.py:39
  93.6 18.9 %collective-permute-start.5 = (bf16[1,16,256]{2,1,0:T(8,128)(2,1)S(1)}, bf16[1,16,256]{2,1,0:T(8,128)(2,1)S(1)}, u32[]{:S(2)}, u32[]{:S(2)}) collective-permute-start(bf16[1,16,256]{2,1,0:T(8,128)(2,1)S(1)} %convert_element_type.102), channel_id=1, source_target_pairs={{0,6},{1,7},{2,4},{3,5},{4,2},{5,3},{6,0},{7,1},{8,14},{9,15},{10,... | collective-permute-start | bytes 24584 | tf_op jit(solution)/shard_map/ppermute | solution.py:39
  96.6 22.9 %collective-permute-start.6 = (bf16[1,16,256]{2,1,0:T(8,128)(2,1)S(1)}, bf16[1,16,256]{2,1,0:T(8,128)(2,1)S(1)}, u32[]{:S(2)}, u32[]{:S(2)}) collective-permute-start(bf16[1,16,256]{2,1,0:T(8,128)(2,1)S(1)} %convert_element_type.102), channel_id=1, source_target_pairs={{0,7},{1,6},{2,5},{3,4},{4,3},{5,2},{6,1},{7,0},{8,15},{9,14},{10,... | collective-permute-start | bytes 24584 | tf_op jit(solution)/shard_map/ppermute | solution.py:39
  101.4 20.1 %collective-permute-start.7 = (bf16[1,16,256]{2,1,0:T(8,128)(2,1)S(1)}, bf16[1,16,256]{2,1,0:T(8,128)(2,1)S(1)}, u32[]{:S(2)}, u32[]{:S(2)}) collective-permute-start(bf16[1,16,256]{2,1,0:T(8,128)(2,1)S(1)} %convert_element_type.102), channel_id=1, source_target_pairs={{0,8},{1,9},{2,10},{3,11},{4,12},{5,13},{6,14},{7,15},{8,0},{9,1},... | collective-permute-start | bytes 24584 | tf_op jit(solution)/shard_map/ppermute | solution.py:39
  104.2 22.7 %collective-permute-start.8 = (bf16[1,16,256]{2,1,0:T(8,128)(2,1)S(1)}, bf16[1,16,256]{2,1,0:T(8,128)(2,1)S(1)}, u32[]{:S(2)}, u32[]{:S(2)}) collective-permute-start(bf16[1,16,256]{2,1,0:T(8,128)(2,1)S(1)} %convert_element_type.102), channel_id=1, source_target_pairs={{0,9},{1,8},{2,11},{3,10},{4,13},{5,12},{6,15},{7,14},{8,1},{9,0},... | collective-permute-start | bytes 24584 | tf_op jit(solution)/shard_map/ppermute | solution.py:39
  110.6 18.3 %collective-permute-start.9 = (bf16[1,16,256]{2,1,0:T(8,128)(2,1)S(1)}, bf16[1,16,256]{2,1,0:T(8,128)(2,1)S(1)}, u32[]{:S(2)}, u32[]{:S(2)}) collective-permute-start(bf16[1,16,256]{2,1,0:T(8,128)(2,1)S(1)} %convert_element_type.102), channel_id=1, source_target_pairs={{0,10},{1,11},{2,8},{3,9},{4,14},{5,15},{6,12},{7,13},{8,2},{9,3},... | collective-permute-start | bytes 24584 | tf_op jit(solution)/shard_map/ppermute | solution.py:39
  112.5 21.6 %collective-permute-start.10 = (bf16[1,16,256]{2,1,0:T(8,128)(2,1)S(1)}, bf16[1,16,256]{2,1,0:T(8,128)(2,1)S(1)}, u32[]{:S(2)}, u32[]{:S(2)}) collective-permute-start(bf16[1,16,256]{2,1,0:T(8,128)(2,1)S(1)} %convert_element_type.102), channel_id=1, source_target_pairs={{0,11},{1,10},{2,9},{3,8},{4,15},{5,14},{6,13},{7,12},{8,3},{9,2},... | collective-permute-start | bytes 24584 | tf_op jit(solution)/shard_map/ppermute | solution.py:39
  119.6 14.6 %collective-permute-start.11 = (bf16[1,16,256]{2,1,0:T(8,128)(2,1)S(1)}, bf16[1,16,256]{2,1,0:T(8,128)(2,1)S(1)}, u32[]{:S(2)}, u32[]{:S(2)}) collective-permute-start(bf16[1,16,256]{2,1,0:T(8,128)(2,1)S(1)} %convert_element_type.102), channel_id=1, source_target_pairs={{0,12},{1,13},{2,14},{3,15},{4,8},{5,9},{6,10},{7,11},{8,4},{9,5},... | collective-permute-start | bytes 24584 | tf_op jit(solution)/shard_map/ppermute | solution.py:39
  121.5 12.6 %collective-permute-start.12 = (bf16[1,16,256]{2,1,0:T(8,128)(2,1)S(1)}, bf16[1,16,256]{2,1,0:T(8,128)(2,1)S(1)}, u32[]{:S(2)}, u32[]{:S(2)}) collective-permute-start(bf16[1,16,256]{2,1,0:T(8,128)(2,1)S(1)} %convert_element_type.102), channel_id=1, source_target_pairs={{0,13},{1,12},{2,15},{3,14},{4,9},{5,8},{6,11},{7,10},{8,5},{9,4},... | collective-permute-start | bytes 24584 | tf_op jit(solution)/shard_map/ppermute | solution.py:39
  126.9 7.3 %collective-permute-start.13 = (bf16[1,16,256]{2,1,0:T(8,128)(2,1)S(1)}, bf16[1,16,256]{2,1,0:T(8,128)(2,1)S(1)}, u32[]{:S(2)}, u32[]{:S(2)}) collective-permute-start(bf16[1,16,256]{2,1,0:T(8,128)(2,1)S(1)} %convert_element_type.102), channel_id=1, source_target_pairs={{0,14},{1,15},{2,12},{3,13},{4,10},{5,11},{6,8},{7,9},{8,6},{9,7},... | collective-permute-start | bytes 24584 | tf_op jit(solution)/shard_map/ppermute | solution.py:39
  128.9 6.6 %collective-permute-start.14 = (bf16[1,16,256]{2,1,0:T(8,128)(2,1)S(1)}, bf16[1,16,256]{2,1,0:T(8,128)(2,1)S(1)}, u32[]{:S(2)}, u32[]{:S(2)}) collective-permute-start(bf16[1,16,256]{2,1,0:T(8,128)(2,1)S(1)} %convert_element_type.102), channel_id=1, source_target_pairs={{0,15},{1,14},{2,13},{3,12},{4,11},{5,10},{6,9},{7,8},{8,7},{9,6},... | collective-permute-start | bytes 24584 | tf_op jit(solution)/shard_map/ppermute | solution.py:39
  136.0 7.3 %copy-start.3 = (bf16[16,64,128]{2,1,0:T(8,128)(2,1)S(1)}, bf16[16,64,128]{2,1,0:T(8,128)(2,1)}, u32[]{:S(2)}) copy-start(bf16[16,64,128]{2,1,0:T(8,128)(2,1)} %param.9) | copy-start | bytes 786436
Sparse Core Ops, SparseCore 0:
  9.5 65.3 all-gather.1
